TPU v7x, 256 devices: a whole 4x4x8 slice. The times are simulated.
256 devices in a mesh: seq: 32 (over z, x), head: 8 (over y, core).
Axes of the slice: x: 4, y: 4, z: 8, core: 2. Of those that a mesh axis runs over, the one named last changes fastest.
Arguments:
- queries: bfloat16 [16384, 4096], P('seq', 'head'), may hold values from -6 to 6
- key_rows: bfloat16 [16384, 4096], P('seq', 'head'), may hold values from -6 to 6
- value_rows: bfloat16 [16384, 4096], P('seq', 'head'), may hold values from -18 to 18
- out_grad: bfloat16 [16384, 4096], P('seq', 'head'), may hold values from -6 to 6
- log_decay: float32 [32, 16384], P('head', 'seq'), may hold values from -0.6 to 0
Outputs:
- query_gradient: bfloat16 [16384, 4096], P('seq', 'head')
- key_grad: bfloat16 [16384, 4096], P('seq', 'head')
- value_grad: bfloat16 [16384, 4096], P('seq', 'head')
All inputs are finite; a program needn't handle non-finite values.
Results may differ from a plain program's by a relative error of at most 0.006.
Values sent between devices are 32-bit elements; how exact they have to be, the bound alone decides.
No kernel may reach another device: no remote copies, remote signals or barrier semaphores. Data moves between devices by JAX's collectives and lax.ppermute only.
A program may use at most 64 MiB of HBM per device.

v0:
```python
import jax
import jax.numpy as jnp
from jax import lax
from jax.sharding import PartitionSpec as P

HEAD_COUNT = 32
DH = 128
BLOCK = 128
epsilon = 1e-06
highest = lax.Precision.HIGHEST


def shards(queries, key_rows, value_rows, out_grad, log_decay):
    tok_rows, row_width = queries.shape
    heads_dev = log_decay.shape[0]
    head_size = row_width // heads_dev
    blocks = tok_rows // BLOCK
    total_width = HEAD_COUNT * DH
    block_shape = (blocks, BLOCK, heads_dev, head_size)
    query_block_rows = queries.reshape(block_shape)
    key_blocks = key_rows.reshape(block_shape)
    value_block_rows = value_rows.reshape(block_shape)
    grad_blocks = out_grad.reshape(block_shape)
    decay_blocks = jnp.transpose(log_decay.reshape(heads_dev, blocks, BLOCK), (1, 2, 0))
    inside_block_mask = jnp.cumsum(decay_blocks, axis=1)
    totals = inside_block_mask[:, -1, :]
    before = jnp.cumsum(totals, axis=0) - totals
    shard_total = jnp.sum(totals, axis=0)
    token_positions = jnp.arange(BLOCK)
    causal = (token_positions[:, None] >= token_positions[None, :]).astype(jnp.float32)
    within_heads = jnp.transpose(inside_block_mask, (0, 2, 1))
    exponent = within_heads[:, :, :, None] - within_heads[:, :, None, :]
    decay_mask = jnp.exp(jnp.minimum(exponent, 0.0)) * causal
    scores = jnp.einsum(
        "nihd,njhd->nhij", query_block_rows, key_blocks, preferred_element_type=jnp.float32
    )
    attention_weights = (scores * decay_mask).astype(jnp.bfloat16)
    intra_out = jnp.einsum(
        "nhij,njhd->nihd", attention_weights, value_block_rows, preferred_element_type=jnp.float32
    )
    to_end = jnp.exp(totals[:, None, :] - inside_block_mask)
    keys_scaled = (to_end[..., None] * key_blocks).astype(jnp.bfloat16)
    block_terms = jnp.einsum(
        "njhd,njhe->nhde", keys_scaled, value_block_rows, preferred_element_type=jnp.float32
    )
    block_ids = jnp.arange(blocks)
    earlier_blocks = (block_ids[:, None] > block_ids[None, :]).astype(jnp.float32)
    forward_exp = before[:, None, :] - before[None, :, :] - totals[None, :, :]
    forward_mix = jnp.exp(jnp.minimum(forward_exp, 0.0)) * earlier_blocks[:, :, None]
    local_states = jnp.einsum("nmh,mhde->nhde", forward_mix, block_terms, precision=highest)
    shard_state = jnp.einsum(
        "mh,mhde->hde",
        jnp.exp(shard_total[None, :] - before - totals),
        block_terms,
        precision=highest,
    )
    all_totals, all_states = (
        lax.all_gather(shard_total[None], "seq", axis=0, tiled=True),
        lax.all_gather(shard_state[None], "seq", axis=0, tiled=True),
    )
    seq_ranks = lax.axis_size("seq")
    my_rank = lax.axis_index("seq")
    starts = jnp.cumsum(all_totals, axis=0) - all_totals
    my_start = lax.dynamic_index_in_dim(starts, my_rank, 0, keepdims=False)
    rank_ids = jnp.arange(seq_ranks)
    reach_log = my_start[None, :] - starts - all_totals
    mixing = jnp.exp(jnp.minimum(reach_log, 0.0)) * (rank_ids < my_rank)[:, None].astype(
        jnp.float32
    )
    incoming = jnp.einsum("rh,rhde->hde", mixing, all_states, precision=highest)
    states = local_states + jnp.exp(before)[:, :, None, None] * incoming[None]
    backward_state = states.astype(jnp.bfloat16)
    inter_out = jnp.einsum(
        "nihd,nhde->nihe", query_block_rows, backward_state, preferred_element_type=jnp.float32
    )
    attention_output = intra_out + jnp.exp(inside_block_mask)[..., None] * inter_out
    square = jnp.sum(attention_output * attention_output, axis=(2, 3))
    square_total = lax.psum(square, "head")
    inv_rms = lax.rsqrt(square_total / total_width + epsilon)
    normed = attention_output * inv_rms[:, :, None, None]
    cross_local = jnp.sum(grad_blocks.astype(jnp.float32) * normed, axis=(2, 3))
    cross_total = lax.psum(cross_local, "head")
    mean_cross = cross_total / total_width
    attention_gradient = (
        inv_rms[:, :, None, None]
        * (grad_blocks.astype(jnp.float32) - normed * mean_cross[:, :, None, None])
    ).astype(jnp.bfloat16)
    score_gradient = jnp.einsum(
        "nihe,njhe->nhij", attention_gradient, value_block_rows, preferred_element_type=jnp.float32
    )
    grad_probs = (score_gradient * decay_mask).astype(jnp.bfloat16)
    query_gradient = jnp.einsum(
        "nhij,njhd->nihd", grad_probs, key_blocks, preferred_element_type=jnp.float32
    )
    query_gradient = query_gradient + jnp.exp(inside_block_mask)[..., None] * jnp.einsum(
        "nihe,nhde->nihd", attention_gradient, backward_state, preferred_element_type=jnp.float32
    )
    key_intra = jnp.einsum(
        "nhij,nihd->njhd", grad_probs, query_block_rows, preferred_element_type=jnp.float32
    )
    value_within_block = jnp.einsum(
        "nhij,nihe->njhe", attention_weights, attention_gradient, preferred_element_type=jnp.float32
    )
    scaled_query_rows = (jnp.exp(inside_block_mask)[..., None] * query_block_rows).astype(
        jnp.bfloat16
    )
    backward_terms = jnp.einsum(
        "nihd,nihe->nhde", scaled_query_rows, attention_gradient, preferred_element_type=jnp.float32
    )
    later_blocks = (block_ids[:, None] < block_ids[None, :]).astype(jnp.float32)
    backward_exp = before[None, :, :] - before[:, None, :] - totals[:, None, :]
    backward_mix = jnp.exp(jnp.minimum(backward_exp, 0.0)) * later_blocks[:, :, None]
    local_back = jnp.einsum("nmh,mhde->nhde", backward_mix, backward_terms, precision=highest)
    shard_back = jnp.einsum("mh,mhde->hde", jnp.exp(before), backward_terms, precision=highest)
    shard_piece = lax.all_gather(shard_back[None], "seq", axis=0, tiled=True)
    piece_rows = shard_piece.shape[0]
    piece_ranks = jnp.arange(piece_rows)
    reach_log = starts - my_start[None, :] - shard_total[None, :]
    mixing = jnp.exp(jnp.minimum(reach_log, 0.0)) * (piece_ranks > my_rank)[:, None].astype(
        jnp.float32
    )
    later_state = jnp.einsum("rh,rhde->hde", mixing, shard_piece, precision=highest)
    back_states = (
        local_back
        + jnp.exp(shard_total[None, :] - before - totals)[:, :, None, None] * later_state[None]
    )
    back_b = back_states.astype(jnp.bfloat16)
    key_grad = key_intra + to_end[..., None] * jnp.einsum(
        "njhe,nhde->njhd", value_block_rows, back_b, preferred_element_type=jnp.float32
    )
    value_grad = value_within_block + to_end[..., None] * jnp.einsum(
        "njhd,nhde->njhe", key_blocks, back_b, preferred_element_type=jnp.float32
    )
    return (
        query_gradient.reshape(tok_rows, row_width).astype(jnp.bfloat16),
        key_grad.reshape(tok_rows, row_width).astype(jnp.bfloat16),
        value_grad.reshape(tok_rows, row_width).astype(jnp.bfloat16),
    )


def solution(mesh):
    return jax.shard_map(
        shards,
        mesh=mesh,
        in_specs=(
            P("seq", "head"),
            P("seq", "head"),
            P("seq", "head"),
            P("seq", "head"),
            P("head", "seq"),
        ),
        out_specs=(P("seq", "head"), P("seq", "head"), P("seq", "head")),
        check_vma=False,
    )
```

profile of v0, /device:TPU:1, one launch (start us, length us, event | category | flops | bytes accessed | tf_op | source)
XLA Modules:
  0.0 287.0 jit_solution(773826581241886380)
XLA Ops:
  7.2 0.0 all-gather.6.cloned.1.call-start
  7.2 0.9 copy.151
  8.2 0.3 reduce_window_sum.35
  8.5 0.1 subtract_exponential_fusion
  8.6 0.1 copy.132
  8.7 0.1 copy.93
  8.8 1.2 reshape.130
  10.0 1.2 reshape.132
  11.2 0.9 fusion.27
  12.1 1.1 copy-done.4
  13.2 3.1 %fusion.24 = f32[4,1,128,128]{3,1,2,0:T(1,128)} fusion(f32[4,4,1,1]{0,2,3,1:T(1,128)S(1)} %copy.132, f32[4,4,128,128]{3,2,1,0:T(8,128)S(1)} %fusion.27), kind=kOutput, calls=%fused_computation.42 | convolution fusion | flops 3145728 | bytes 1310784 | tf_op jit(solution)/shard_map/mh,mhde->hde/dot_general | solution.py:51
  16.3 0.0 all-gather.8.cloned.1.call-start
  16.3 0.1 copy.99
  16.4 0.1 copy.100
  16.5 1.3 dynamic-slice
  18.4 0.2 dynamic-update-slice
  18.7 64.9 %all-reduce = f32[128]{0:T(128)S(1)} all-reduce(f32[128]{0:T(128)S(1)} %dynamic-update-slice), channel_id=2, replica_groups=mesh['seq'=32,'head'=8] {'seq'}, use_global_device_ids=true, to_apply=%add | all-reduce | flops 128 | bytes 1024
  83.6 0.1 reshape.134
  83.7 0.1 reduce_window_sum.38
  83.8 0.1 multiply_bitcast_fusion
  83.8 0.1 copy.134
  83.9 0.1 copy.102
  84.0 0.1 copy.98
  84.1 0.1 copy.89
  84.2 0.1 reshape.129
  84.4 0.3 copy.116
  84.7 0.1 copy.92
  84.8 1.3 reshape.133
  86.1 1.6 copy.106
  87.7 0.1 copy.143
  87.8 0.6 fusion.17
  88.4 0.8 copy-done.8
  89.2 1.5 convolution_bitcast_fusion.9
  90.7 26.8 %all-gather.6.cloned.1.call-done = f32[128,128,128]{2,1,0:T(8,128)} async-done(((f32[4,128,128]{2,1,0:T(8,128)}), f32[128,128,128]{2,1,0:T(8,128)}) %all-gather.6.cloned.1.call-update) | async-done | bytes 8388624 | tf_op jit(solution)/shard_map/all_gather | solution.py:59
  117.5 12.2 %fusion.2 = f32[4,1,128,128]{3,1,2,0:T(1,128)S(1)} fusion(f32[32,4,1,1]{0,2,3,1:T(1,128)S(1)} %copy.134, f32[32,4,128,128]{3,2,1,0:T(8,128)} %bitcast.121), kind=kOutput, calls=%fused_computation.2 | convolution fusion | flops 25165824 | bytes 8651264 | tf_op jit(solution)/shard_map/rh,rhde->hde/dot_general | solution.py:70
  129.7 2.7 fusion.18
  132.4 1.6 multiply_reduce_fusion.1
  134.1 13.2 %psum.14 = f32[4,128]{1,0:T(4,128)S(1)} all-reduce(f32[4,128]{1,0:T(4,128)S(1)} %get-tuple-element.13), channel_id=1, replica_groups=mesh['seq'=32,'head'=8] {'head'}, use_global_device_ids=true, to_apply=%region_5.6 | all-reduce | flops 512 | bytes 4096 | tf_op jit(solution)/shard_map/psum | solution.py:78
  147.3 0.1 multiply_reduce_fusion
  147.4 14.1 %psum.15 = f32[4,128]{1,0:T(4,128)S(1)} all-reduce(f32[4,128]{1,0:T(4,128)S(1)} %multiply_reduce_fusion), channel_id=1, replica_groups=mesh['seq'=32,'head'=8] {'head'}, use_global_device_ids=true, to_apply=%region_7.8 | all-reduce | flops 512 | bytes 4096 | tf_op jit(solution)/shard_map/psum | solution.py:82
  161.5 0.2 multiply_convert_fusion.1
  161.7 0.8 copy-done
  162.5 1.6 fusion.28
  164.1 3.1 %fusion.21 = f32[4,1,128,128]{3,1,2,0:T(1,128)} fusion(f32[4,4,1,1]{0,2,3,1:T(1,128)S(1)} %copy.143, f32[4,4,128,128]{3,2,1,0:T(8,128)S(1)} %fusion.28), kind=kOutput, calls=%fused_computation.39 | convolution fusion | flops 3145728 | bytes 1310784 | tf_op jit(solution)/shard_map/mh,mhde->hde/dot_general | solution.py:114
  167.2 0.1 copy.120
  167.3 0.1 copy.145
  167.4 1.6 fusion.19
  169.1 0.8 copy-done.9
  169.9 0.5 convolution_bitcast_fusion.6
  170.4 2.3 fusion.14
  172.7 2.2 copy.113
  174.9 2.0 copy.196
  176.9 2.6 convolution_bitcast_fusion.2
  179.5 2.5 convolution_bitcast_fusion.4
  182.0 77.0 %all-gather.8.cloned.1.call-done = f32[128,128,128]{2,1,0:T(8,128)} async-done(((f32[4,128,128]{2,1,0:T(8,128)}), f32[128,128,128]{2,1,0:T(8,128)}) %all-gather.8.cloned.1.call-update) | async-done | bytes 8388624 | tf_op jit(solution)/shard_map/all_gather | solution.py:115
  259.0 12.3 %fusion = f32[4,1,128,128]{3,1,2,0:T(1,128)S(1)} fusion(f32[32,4,1,1]{0,2,3,1:T(1,128)S(1)} %copy.145, f32[32,4,128,128]{3,2,1,0:T(8,128)} %bitcast.122), kind=kOutput, calls=%fused_computation | convolution fusion | flops 25165824 | bytes 8651264 | tf_op jit(solution)/shard_map/rh,rhde->hde/dot_general | solution.py:122
  271.3 2.6 fusion.20
  273.9 0.4 copy.126
  274.3 1.7 fusion.15
  276.0 0.4 copy.129
  276.4 0.9 copy.194
  277.3 1.6 fusion.16
  278.9 0.4 copy.124
  279.3 0.9 copy.195
  (36 shorter events, 0.2 us)
Async XLA Ops:
  7.2 77.1 %copy-start.11 = (bf16[512,512]{1,0:T(8,128)(2,1)S(1)}, bf16[512,512]{1,0:T(8,128)(2,1)}, u32[]{:S(2)}) copy-start(bf16[512,512]{1,0:T(8,128)(2,1)} %param.5) | copy-start | bytes 1572868
  7.2 77.6 %copy-start.10 = (bf16[512,512]{1,0:T(8,128)(2,1)S(1)}, bf16[512,512]{1,0:T(8,128)(2,1)}, u32[]{:S(2)}) copy-start(bf16[512,512]{1,0:T(8,128)(2,1)} %param.8) | copy-start | bytes 1572868
  7.2 110.3 %all-gather.6.cloned.1.call-start = ((), (), s32[]{:S(2)}) async-start(), calls=%async_computation | async-start | bytes 8650752 | tf_op jit(solution)/shard_map/all_gather | solution.py:59
  12.1 1.1 copy-start.4
  16.3 242.7 %all-gather.8.cloned.1.call-start = ((), (), s32[]{:S(2)}) async-start(), calls=%async_computation.1 | async-start | bytes 8650752 | tf_op jit(solution)/shard_map/all_gather | solution.py:115
  84.7 45.0 %copy-start.2 = (bf16[4,128,4,128]{1,3,2,0:T(8,128)(2,1)}, bf16[4,128,4,128]{1,3,2,0:T(8,128)(2,1)S(1)}, u32[]{:S(2)}) copy-start(bf16[4,128,4,128]{1,3,2,0:T(8,128)(2,1)S(1)} %copy.116) | copy-start | bytes 1572868
  88.4 0.8 copy-start.8
  117.5 12.2 %copy-start.5 = (f32[4,4,128,128]{3,2,1,0:T(8,128)S(1)}, f32[4,4,128,128]{3,2,1,0:T(8,128)}, u32[]{:S(2)}) copy-start(f32[4,4,128,128]{3,2,1,0:T(8,128)} %copy-done.4) | copy-start | bytes 3145732
  117.5 14.9 %copy-start.6 = (f32[4,128,4,128]{1,3,2,0:T(8,128)S(1)}, f32[4,128,4,128]{1,3,2,0:T(8,128)}, u32[]{:S(2)}) copy-start(f32[4,128,4,128]{1,3,2,0:T(8,128)} %convolution_bitcast_fusion.9) | copy-start | bytes 3145732
  132.4 1.7 copy-start.7
  161.7 0.8 copy-start
  162.5 17.0 %copy-start.3 = (bf16[4,128,4,128]{1,3,2,0:T(8,128)(2,1)S(1)}, bf16[4,128,4,128]{1,3,2,0:T(8,128)(2,1)}, u32[]{:S(2)}) copy-start(bf16[4,128,4,128]{1,3,2,0:T(8,128)(2,1)} %copy-done.2) | copy-start | bytes 1572868
  164.1 12.7 %copy-start.1 = (bf16[4,128,4,128]{1,3,2,0:T(8,128)(2,1)S(1)}, bf16[4,128,4,128]{1,3,2,0:T(8,128)(2,1)}, u32[]{:S(2)}) copy-start(bf16[4,128,4,128]{1,3,2,0:T(8,128)(2,1)} %copy-done) | copy-start | bytes 1572868
  169.0 0.8 copy-start.9
Sparse Core Ops, SparseCore 0:
  16.4 101.0 all-gather.5
  167.3 91.5 all-gather.7
where the time goes:
time: 288 us; the launch traced here: 287 us
  waiting for transfers between devices  104 us (36%)
  blocking collectives  92.1 us (32%)
  matrix products  55.1 us (19%)
  local copies, waits for them, and re-layouts  19.9 us (7%)
  between operations  15 us (5%)
    all_gather x1, waiting for transfers between devices, shards(): shard_piece = lax.all_gather(shard_back[None], 'seq', axis=0, tiled=True)  77 us
    unnamed x1, blocking collectives  64.9 us
    all_gather x1, waiting for transfers between devices, shards(): lax.all_gather(shard_state[None], 'seq', axis=0, tiled=True)  26.8 us
    psum x1, blocking collectives, shards(): cross_total = lax.psum(cross_local, 'head')  14.1 us
    psum x1, blocking collectives, shards(): square_total = lax.psum(square, 'head')  13.2 us
    dot_general x1, matrix products, shards(): jnp.einsum('rh,rhde->hde', mixing, shard_piece, precision=highest)  12.3 us
    dot_general x1, matrix products, shards(): incoming = jnp.einsum('rh,rhde->hde', mixing, all_states, precision=highest)  12.2 us
    unnamed x30, local copies, waits for them, and re-layouts  8.71 us
  transfers between devices with their start and end apart: 2, of which 2 were waited for; matrix products, arithmetic and copies ran while one was open for 8% of the time, Pallas kernels for 0%

commit v1 on v0

--- a/solution.py
+++ b/solution.py
@@ -79,7 +79,7 @@
     inv_rms = lax.rsqrt(square_total / total_width + epsilon)
     normed = attention_output * inv_rms[:, :, None, None]
     cross_local = jnp.sum(grad_blocks.astype(jnp.float32) * normed, axis=(2, 3))
-    cross_total = lax.psum(cross_local, "head")
+    cross_total = jnp.sum(lax.all_gather(cross_local, "head"), axis=0)
     mean_cross = cross_total / total_width
     attention_gradient = (
         inv_rms[:, :, None, None]

time: 288 us -> 288 us (level)
    psum x1 -> x0, blocking collectives: 14.1 us -> none  [shards(): cross_total = lax.psum(cross_local, 'head')]
    all_gather x0 -> x1, blocking collectives: none -> 13.4 us  [shards(): cross_total = jnp.sum(lax.all_gather(cross_local, 'head'), axis=0)]
where the time goes in v1:
time: 288 us
  waiting for transfers between devices  105 us (36%)
  blocking collectives  91.5 us (32%)
  matrix products  54.9 us (19%)
  local copies, waits for them, and re-layouts  19.9 us (7%)
  between operations  15 us (5%)
    all_gather x1, waiting for transfers between devices, shards(): shard_piece = lax.all_gather(shard_back[None], 'seq', axis=0, tiled=True)  78.4 us
    unnamed x1, blocking collectives  64.9 us
    all_gather x1, waiting for transfers between devices, shards(): lax.all_gather(shard_state[None], 'seq', axis=0, tiled=True)  26.8 us
    all_gather x1, blocking collectives, shards(): cross_total = jnp.sum(lax.all_gather(cross_local, 'head'), axis=0)  13.4 us
    psum x1, blocking collectives, shards(): square_total = lax.psum(square, 'head')  13.2 us
    dot_general x1, matrix products, shards(): incoming = jnp.einsum('rh,rhde->hde', mixing, all_states, precision=highest)  12.2 us
    dot_general x1, matrix products, shards(): jnp.einsum('rh,rhde->hde', mixing, shard_piece, precision=highest)  12 us
    unnamed x30, local copies, waits for them, and re-layouts  8.69 us
  transfers between devices with their start and end apart: 2, of which 2 were waited for; matrix products, arithmetic and copies ran while one was open for 8% of the time, Pallas kernels for 0%

profile of v1, /device:TPU:1, one launch (start us, length us, event | category | flops | bytes accessed | tf_op | source)
XLA Modules:
  0.0 287.6 jit_solution(13130188976721603181)
XLA Ops:
  7.2 0.0 all-gather.8.cloned.1.call-start
  7.2 0.9 copy.151
  8.2 0.3 reduce_window_sum.35
  8.5 0.1 subtract_exponential_fusion
  8.6 0.1 copy.132
  8.7 0.1 copy.93
  8.8 1.2 reshape.132
  10.0 1.2 reshape.134
  11.2 0.9 fusion.27
  12.1 1.1 copy-done.4
  13.2 3.1 %fusion.24 = f32[4,1,128,128]{3,1,2,0:T(1,128)} fusion(f32[4,4,1,1]{0,2,3,1:T(1,128)S(1)} %copy.132, f32[4,4,128,128]{3,2,1,0:T(8,128)S(1)} %fusion.27), kind=kOutput, calls=%fused_computation.42 | convolution fusion | flops 3145728 | bytes 1310784 | tf_op jit(solution)/shard_map/mh,mhde->hde/dot_general | solution.py:51
  16.3 0.0 all-gather.10.cloned.1.call-start
  16.3 0.1 copy.99
  16.4 0.1 copy.100
  16.5 1.3 dynamic-slice
  18.4 0.2 dynamic-update-slice
  18.7 64.9 %all-reduce = f32[128]{0:T(128)S(1)} all-reduce(f32[128]{0:T(128)S(1)} %dynamic-update-slice), channel_id=2, replica_groups=mesh['seq'=32,'head'=8] {'seq'}, use_global_device_ids=true, to_apply=%add | all-reduce | flops 128 | bytes 1024
  83.6 0.1 reshape.136
  83.7 0.1 reduce_window_sum.38
  83.8 0.1 multiply_bitcast_fusion
  83.8 0.1 copy.134
  83.9 0.1 copy.102
  84.0 0.1 copy.98
  84.1 0.1 copy.89
  84.2 0.1 reshape.131
  84.4 0.3 copy.116
  84.7 0.1 copy.92
  84.8 1.3 reshape.135
  86.1 1.6 copy.106
  87.7 0.1 copy.143
  87.8 0.6 fusion.17
  88.4 0.8 copy-done.8
  89.2 1.5 convolution_bitcast_fusion.9
  90.7 26.8 %all-gather.8.cloned.1.call-done = f32[128,128,128]{2,1,0:T(8,128)} async-done(((f32[4,128,128]{2,1,0:T(8,128)}), f32[128,128,128]{2,1,0:T(8,128)}) %all-gather.8.cloned.1.call-update) | async-done | bytes 8388624 | tf_op jit(solution)/shard_map/all_gather | solution.py:59
  117.5 12.2 %fusion.2 = f32[4,1,128,128]{3,1,2,0:T(1,128)S(1)} fusion(f32[32,4,1,1]{0,2,3,1:T(1,128)S(1)} %copy.134, f32[32,4,128,128]{3,2,1,0:T(8,128)} %bitcast.122), kind=kOutput, calls=%fused_computation.2 | convolution fusion | flops 25165824 | bytes 8651264 | tf_op jit(solution)/shard_map/rh,rhde->hde/dot_general | solution.py:70
  129.7 2.7 fusion.18
  132.4 1.6 multiply_reduce_fusion.1
  134.1 13.2 %psum.7 = f32[4,128]{1,0:T(4,128)S(1)} all-reduce(f32[4,128]{1,0:T(4,128)S(1)} %get-tuple-element.13), channel_id=1, replica_groups=mesh['seq'=32,'head'=8] {'head'}, use_global_device_ids=true, to_apply=%region_5.6 | all-reduce | flops 512 | bytes 4096 | tf_op jit(solution)/shard_map/psum | solution.py:78
  147.3 0.1 multiply_reduce_fusion
  147.4 13.4 %all-gather.4 = f32[8,4,128]{2,1,0:T(4,128)S(1)} all-gather(f32[1,4,128]{2,1,0:T(4,128)S(1)} %bitcast.144), channel_id=4, replica_groups=mesh['seq'=32,'head'=8] {'head'}, dimensions={0}, use_global_device_ids=true | all-gather | bytes 18432 | tf_op jit(solution)/shard_map/all_gather | solution.py:82
  160.9 0.2 multiply_convert_fusion.1
  161.1 0.8 copy-done
  161.9 1.6 fusion.28
  163.5 3.1 %fusion.21 = f32[4,1,128,128]{3,1,2,0:T(1,128)} fusion(f32[4,4,1,1]{0,2,3,1:T(1,128)S(1)} %copy.143, f32[4,4,128,128]{3,2,1,0:T(8,128)S(1)} %fusion.28), kind=kOutput, calls=%fused_computation.39 | convolution fusion | flops 3145728 | bytes 1310784 | tf_op jit(solution)/shard_map/mh,mhde->hde/dot_general | solution.py:114
  166.6 0.1 copy.120
  166.7 0.1 copy.145
  166.8 1.6 fusion.19
  168.4 0.8 copy-done.9
  169.2 0.5 convolution_bitcast_fusion.6
  169.7 2.3 fusion.14
  172.1 2.2 copy.113
  174.3 1.9 copy.196
  176.2 2.6 convolution_bitcast_fusion.2
  178.8 2.5 convolution_bitcast_fusion.4
  181.4 78.4 %all-gather.10.cloned.1.call-done = f32[128,128,128]{2,1,0:T(8,128)} async-done(((f32[4,128,128]{2,1,0:T(8,128)}), f32[128,128,128]{2,1,0:T(8,128)}) %all-gather.10.cloned.1.call-update) | async-done | bytes 8388624 | tf_op jit(solution)/shard_map/all_gather | solution.py:115
  259.7 12.0 %fusion = f32[4,1,128,128]{3,1,2,0:T(1,128)S(1)} fusion(f32[32,4,1,1]{0,2,3,1:T(1,128)S(1)} %copy.145, f32[32,4,128,128]{3,2,1,0:T(8,128)} %bitcast.123), kind=kOutput, calls=%fused_computation | convolution fusion | flops 25165824 | bytes 8651264 | tf_op jit(solution)/shard_map/rh,rhde->hde/dot_general | solution.py:122
  271.8 2.7 fusion.20
  274.5 0.4 copy.126
  274.9 1.7 fusion.15
  276.6 0.4 copy.129
  277.0 0.9 copy.194
  277.9 1.6 fusion.16
  279.5 0.4 copy.124
  279.9 0.9 copy.195
  (37 shorter events, 0.2 us)
Async XLA Ops:
  7.2 77.1 %copy-start.11 = (bf16[512,512]{1,0:T(8,128)(2,1)S(1)}, bf16[512,512]{1,0:T(8,128)(2,1)}, u32[]{:S(2)}) copy-start(bf16[512,512]{1,0:T(8,128)(2,1)} %param.5) | copy-start | bytes 1572868
  7.2 77.6 %copy-start.10 = (bf16[512,512]{1,0:T(8,128)(2,1)S(1)}, bf16[512,512]{1,0:T(8,128)(2,1)}, u32[]{:S(2)}) copy-start(bf16[512,512]{1,0:T(8,128)(2,1)} %param.8) | copy-start | bytes 1572868
  7.2 110.3 %all-gather.8.cloned.1.call-start = ((), (), s32[]{:S(2)}) async-start(), calls=%async_computation | async-start | bytes 8650752 | tf_op jit(solution)/shard_map/all_gather | solution.py:59
  12.1 1.1 copy-start.4
  16.3 243.5 %all-gather.10.cloned.1.call-start = ((), (), s32[]{:S(2)}) async-start(), calls=%async_computation.1 | async-start | bytes 8650752 | tf_op jit(solution)/shard_map/all_gather | solution.py:115
  84.7 45.0 %copy-start.2 = (bf16[4,128,4,128]{1,3,2,0:T(8,128)(2,1)}, bf16[4,128,4,128]{1,3,2,0:T(8,128)(2,1)S(1)}, u32[]{:S(2)}) copy-start(bf16[4,128,4,128]{1,3,2,0:T(8,128)(2,1)S(1)} %copy.116) | copy-start | bytes 1572868
  88.4 0.8 copy-start.8
  117.5 12.2 %copy-start.5 = (f32[4,4,128,128]{3,2,1,0:T(8,128)S(1)}, f32[4,4,128,128]{3,2,1,0:T(8,128)}, u32[]{:S(2)}) copy-start(f32[4,4,128,128]{3,2,1,0:T(8,128)} %copy-done.4) | copy-start | bytes 3145732
  117.5 14.9 %copy-start.6 = (f32[4,128,4,128]{1,3,2,0:T(8,128)S(1)}, f32[4,128,4,128]{1,3,2,0:T(8,128)}, u32[]{:S(2)}) copy-start(f32[4,128,4,128]{1,3,2,0:T(8,128)} %convolution_bitcast_fusion.9) | copy-start | bytes 3145732
  132.4 1.7 copy-start.7
  161.1 0.8 copy-start
  161.9 16.9 %copy-start.3 = (bf16[4,128,4,128]{1,3,2,0:T(8,128)(2,1)S(1)}, bf16[4,128,4,128]{1,3,2,0:T(8,128)(2,1)}, u32[]{:S(2)}) copy-start(bf16[4,128,4,128]{1,3,2,0:T(8,128)(2,1)} %copy-done.2) | copy-start | bytes 1572868
  163.5 12.7 %copy-start.1 = (bf16[4,128,4,128]{1,3,2,0:T(8,128)(2,1)S(1)}, bf16[4,128,4,128]{1,3,2,0:T(8,128)(2,1)}, u32[]{:S(2)}) copy-start(bf16[4,128,4,128]{1,3,2,0:T(8,128)(2,1)} %copy-done) | copy-start | bytes 1572868
  168.4 0.8 copy-start.9
Sparse Core Ops, SparseCore 0:
  16.4 101.0 all-gather.7
  166.7 92.9 all-gather.9
